TPU v7x, 32 devices: a whole 2x2x4 slice. The times are simulated.
32 devices in a mesh: day: 4 (over z), dom: 8 (over y, x, core).
Axes of the slice: x: 2, y: 2, z: 4, core: 2. Of those that a mesh axis runs over, the one named last changes fastest.
Arguments:
- node_states: bfloat16 [16, 2048, 256], P('day', 'dom'), may hold values from -12 to 12
- edge_source: int32 [16, 8192], P('day', 'dom'), may hold values from 0 to 383
- edge_target: int32 [16, 8192], P('day', 'dom'), may hold values from 0 to 255
- halo_rows: int32 [16, 1024], P('day', 'dom'), may hold values from 0 to 255
- halo_count: int32 [16, 8], P('day', 'dom'), may hold values from 1 to 128, 640 in all within a row
- w_message: bfloat16 [256, 256], replicated, may hold values from -0.375 to 0.375
- w_query: bfloat16 [256, 256], replicated, may hold values from -1 to 1, as said below
- w_key: bfloat16 [256, 256], replicated, may hold values from -1 to 1, as said below
- w_value: bfloat16 [256, 256], replicated, may hold values from -0.375 to 0.375
- cotangent: bfloat16 [16, 8, 4, 64, 256], P(None, 'dom', 'day'), may hold values from -6 to 6
Outputs:
- state_grad: float32 [16, 2048, 256], P('day', 'dom')
- grad_message: float32 [256, 256], replicated
- grad_query: float32 [256, 256], replicated
- grad_key: float32 [256, 256], replicated
- grad_value: float32 [256, 256], replicated
Inputs may be any that keep to these rules, and one draw needn't show every extreme that they name: `edge_source`: indices of the extended rows: below 256 a partition's own account, from 256 on a received halo slot. `halo_rows`: rows of the sending partition's own block; repeats allowed. `halo_count`: on every day some partition has all 128 slots live. `w_query`: entries of order 256 ** -0.5. `w_key`: entries of order 256 ** -0.5.
All inputs are finite; a program needn't handle non-finite values. No bound on the sum of `halo_count` on one device may be relied on, other than what follows from the above.
Results may differ from a plain program's by a relative error of at most 0.004.
The roundings to bfloat16 on the way count: a program that leaves them out, or rounds other values in their place, can miss the bound.
Values may be sent and summed in bfloat16 or wider, within the bound.
No kernel may reach another device: no remote copies, remote signals or barrier semaphores. Data moves between devices by JAX's collectives and lax.ppermute only.
A program may use at most 64 MiB of HBM per device.

v0:
```python
import jax
import jax.numpy as jnp
from jax import lax
from jax.sharding import PartitionSpec as P

HEADS = 4


def from_behind(value, axis, steps):
    count = lax.axis_size(axis)
    pairs = [(source, (source + steps) % count) for source in range(count)]
    return lax.ppermute(value, axis, pairs)


def adjacency(sources, targets, count_rows, total_rows):
    target_hot = (targets[:, None] == jnp.arange(count_rows, dtype=jnp.int32)[None, :]).astype(
        jnp.bfloat16
    )
    source_hot = (sources[:, None] == jnp.arange(total_rows, dtype=jnp.int32)[None, :]).astype(
        jnp.bfloat16
    )
    counts = lax.dot_general(
        target_hot, source_hot, (((0,), (0,)), ((), ())), preferred_element_type=jnp.float32
    )
    return counts.astype(jnp.bfloat16)


def gnn_forward(states, received, adjacent, w_message):
    extended = jnp.concatenate([states, received], axis=0)
    neighbours = jnp.dot(adjacent, extended, preferred_element_type=jnp.float32)
    counted = jnp.sum(adjacent.astype(jnp.float32), axis=1)
    inverse = 1.0 / (counted + 1.0)
    aggregate = ((states.astype(jnp.float32) + neighbours) * inverse[:, None]).astype(jnp.bfloat16)
    preact = jnp.dot(aggregate, w_message, preferred_element_type=jnp.float32)
    hidden = (states.astype(jnp.float32) + jax.nn.silu(preact)).astype(jnp.bfloat16)
    return (aggregate, preact, inverse, hidden)


def gnn_backward(upstream, aggregate, preact, inverse, adjacent, w_message):
    count_rows = aggregate.shape[0]
    up_float = upstream.astype(jnp.float32)
    sigmoid_val = jax.nn.sigmoid(preact)
    pre_grad = (up_float * sigmoid_val * (1.0 + preact * (1.0 - sigmoid_val))).astype(jnp.bfloat16)
    message_part = lax.dot_general(
        aggregate, pre_grad, (((0,), (0,)), ((), ())), preferred_element_type=jnp.float32
    )
    agg_grad = lax.dot_general(
        pre_grad, w_message, (((1,), (1,)), ((), ())), preferred_element_type=jnp.float32
    )
    term_grad = agg_grad * inverse[:, None]
    ext_grad = lax.dot_general(
        adjacent.astype(jnp.float32),
        term_grad,
        (((0,), (0,)), ((), ())),
        precision=lax.Precision.HIGHEST,
        preferred_element_type=jnp.float32,
    )
    local_grad = up_float + term_grad + ext_grad[:count_rows]
    halo_grad = ext_grad[count_rows:].astype(jnp.bfloat16)
    return (message_part, local_grad, halo_grad)


def attend(states, upstream, w_query, w_key, w_value):
    steps_all, nodes_here, width = states.shape
    head_dim = width // HEADS
    scale_factor = head_dim ** (-0.5)
    flat = states.reshape(steps_all * nodes_here, width)

    def project(weight):
        return jnp.dot(flat, weight, preferred_element_type=jnp.float32).astype(jnp.bfloat16)

    def splitter(matrix):
        return matrix.reshape(steps_all, nodes_here, HEADS, head_dim).astype(jnp.float32)

    queries = project(w_query)
    key_rows = project(w_key)
    value_rows = project(w_value)
    query_f = splitter(queries)
    key_f = splitter(key_rows)
    value_f = splitter(value_rows)
    scores = jnp.einsum("tnhd,snhd->nhts", query_f, key_f) * scale_factor
    causal = jnp.arange(steps_all)[:, None] >= jnp.arange(steps_all)[None, :]
    scores = jnp.where(causal, scores, -jnp.inf)
    highest = jnp.max(scores, axis=-1, keepdims=True)
    exponent = jnp.exp(scores - highest)
    probs = exponent / jnp.sum(exponent, axis=-1, keepdims=True)
    probs_low = probs.astype(jnp.bfloat16).astype(jnp.float32)
    up_heads = splitter(upstream)
    value_grad = jnp.einsum("nhts,tnhd->snhd", probs_low, up_heads).astype(jnp.bfloat16)
    prob_grad = jnp.einsum("tnhd,snhd->nhts", up_heads, value_f)
    score_grad = (
        probs * (prob_grad - jnp.sum(prob_grad * probs, axis=-1, keepdims=True)) * scale_factor
    ).astype(jnp.bfloat16)
    score_f = score_grad.astype(jnp.float32)
    query_grad = jnp.einsum("nhts,snhd->tnhd", score_f, key_f).astype(jnp.bfloat16)
    key_grad = jnp.einsum("nhts,tnhd->snhd", score_f, query_f).astype(jnp.bfloat16)
    query_flat = query_grad.reshape(steps_all * nodes_here, width)
    key_flat = key_grad.reshape(steps_all * nodes_here, width)
    value_flat = value_grad.reshape(steps_all * nodes_here, width)

    def weight_grad(grad_rows):
        return lax.dot_general(
            flat, grad_rows, (((0,), (0,)), ((), ())), preferred_element_type=jnp.float32
        )

    def input_grad(grad_rows, weight):
        return lax.dot_general(
            grad_rows, weight, (((1,), (1,)), ((), ())), preferred_element_type=jnp.float32
        )

    back = upstream.reshape(steps_all * nodes_here, width).astype(jnp.float32)
    back = (
        back
        + input_grad(query_flat, w_query)
        + input_grad(key_flat, w_key)
        + input_grad(value_flat, w_value)
    )
    back = back.astype(jnp.bfloat16).reshape(steps_all, nodes_here, width)
    return ((weight_grad(query_flat), weight_grad(key_flat), weight_grad(value_flat)), back)


def local(
    node_states,
    edge_source,
    edge_target,
    halo_rows,
    halo_count,
    w_message,
    w_query,
    w_key,
    w_value,
    cotangent,
):
    days_local, node_local, width = node_states.shape
    halo_slots = halo_rows.shape[1]
    live = jnp.arange(halo_slots)[None, :] < halo_count
    picked = jnp.take_along_axis(node_states, halo_rows[:, :, None], axis=1)
    sent = jnp.where(live[:, :, None], picked, jnp.zeros_like(picked))
    received = from_behind(sent, "dom", 1)

    def forward_one(items):
        adjacent = adjacency(items[2], items[3], node_local, node_local + halo_slots)
        aggregate, preact, inverse, hidden = gnn_forward(items[0], items[1], adjacent, w_message)
        return (aggregate, preact, inverse, hidden, adjacent)

    aggregate, preact, inverse, hidden, adjacent = lax.map(
        forward_one, (node_states, received, edge_source, edge_target)
    )
    node_major = lax.all_to_all(hidden, "day", split_axis=1, concat_axis=0, tiled=True)
    upstream = cotangent.reshape(cotangent.shape[0], -1, width)
    attn_grads, back = attend(node_major, upstream, w_query, w_key, w_value)
    back_days = lax.all_to_all(back, "day", split_axis=0, concat_axis=1, tiled=True)

    def backward_one(items):
        return gnn_backward(items[0], items[1], items[2], items[3], items[4], w_message)

    message_parts, local_grad, halo_grad = lax.map(
        backward_one, (back_days, aggregate, preact, inverse, adjacent)
    )
    grad_message = jnp.sum(message_parts, axis=0)
    returned = from_behind(halo_grad, "dom", -1)
    slot_hot = jnp.logical_and(
        halo_rows[:, :, None] == jnp.arange(node_local, dtype=jnp.int32)[None, None, :],
        live[:, :, None],
    ).astype(jnp.bfloat16)
    scattered = jnp.einsum("dsn,dsh->dnh", slot_hot, returned, preferred_element_type=jnp.float32)
    state_grad = local_grad + scattered
    grad_message, grad_query, grad_key, grad_value = lax.psum(
        (grad_message, attn_grads[0], attn_grads[1], attn_grads[2]), ("day", "dom")
    )
    return (state_grad, grad_message, grad_query, grad_key, grad_value)


def solution(mesh):
    return jax.shard_map(
        local,
        mesh=mesh,
        in_specs=(
            P("day", "dom", None),
            P("day", "dom"),
            P("day", "dom"),
            P("day", "dom"),
            P("day", "dom"),
            P(),
            P(),
            P(),
            P(),
            P(None, "dom", "day", None, None),
        ),
        out_specs=(P("day", "dom", None), P(), P(), P(), P()),
        check_vma=False,
    )
```

profile of v0, /device:TPU:0, one launch (start us, length us, event | category | flops | bytes accessed | tf_op | source)
XLA Modules:
  0.0 277.3 jit_solution(9602864403409959612)
XLA Ops:
  8.7 7.0 %gather_fusion = bf16[512,256]{1,0:T(8,128)(2,1)S(1)} fusion(bf16[4,256,256]{2,1,0:T(8,128)(2,1)} %param.14, s32[512]{0:T(512)S(1)} %fusion.70), kind=kCustom, calls=%fused_computation | custom fusion | bytes 528384 | tf_op jit(solution)/shard_map/jit(take_along_axis)/gather | solution.py:137
  16.4 6.9 %collective-permute-done = bf16[4,128,256]{2,1,0:T(8,128)(2,1)S(1)} collective-permute-done((bf16[4,128,256]{2,1,0:T(8,128)(2,1)S(1)}, bf16[4,128,256]{2,1,0:T(8,128)(2,1)S(1)}, u32[]{:S(2)}, u32[]{:S(2)}) %collective-permute-start) | collective-permute-done | bytes 262176 | tf_op jit(solution)/shard_map/ppermute | solution.py:12
  23.4 12.2 %while.34 = (s32[]{:T(128)}, bf16[4,256,256]{2,1,0:T(8,128)(2,1)S(1)}, f32[4,256,256]{2,1,0:T(8,128)S(1)}, f32[4,256]{1,0:T(4,128)S(1)}, bf16[4,256,256]{2,1,0:T...) while((s32[]{:T(128)}, ...), condition=%wide.region_2.3_spmd.clone, body=%wide.region_0.2_spmd.sunk.clone | while | flops 287277312 | bytes 3111561 | solution.py:146
  36.9 5.6 %all-to-all-start = ((bf16[4,256,256]{2,0,1:T(4,128)(2,1)}), bf16[4,256,256]{2,0,1:T(4,128)(2,1)S(1)}, u32[]{:S(2)}, u32[]{:S(2)}) async-start(bf16[4,256,256]{2,0,1:T(4,128)(2,1)} %copy.52), calls=%async_computation | async-start | bytes 1048576 | tf_op jit(solution)/shard_map/all_to_all | solution.py:149
  42.9 12.5 %all-to-all-done = bf16[4,256,256]{2,0,1:T(4,128)(2,1)S(1)} async-done(((bf16[4,256,256]{2,0,1:T(4,128)(2,1)}), bf16[4,256,256]{2,0,1:T(4,128)(2,1)S(1)}, u32[]{:S(2)}, u32[]{:S(2)}) %all-to-all-start) | async-done | bytes 524320 | tf_op jit(solution)/shard_map/all_to_all | solution.py:149
  59.6 2.6 fusion.52
  62.3 4.9 %fusion.77 = (f32[64,4,16]{2,1,0:T(4,128)S(1)}, f32[64,4,16,16]{2,3,1,0:T(8,128)}) fusion(pred[16,16]{0,1:T(8,128)(4,1)S(1)} %iota_compare_fusion.7, bf16[16,64,4,64]{3,2,1,0:T(4,128)(2,1)} %reshape.99, bf16[16,64,4,64]{3,2,1,0:T(4,128)(2,1)} %reshape.100), kind=kOutput, calls=%fused_computation.119 | convolution fusion | flops 8650767 | bytes 1327360 | tf_op jit(solution)/shard_map/sub | solution.py:85
  67.2 5.8 %fusion.50 = bf16[16,64,4,64]{3,0,2,1:T(8,128)(2,1)} fusion(f32[64,4,16,16]{3,2,1,0:T(8,128)} %fusion.52, bf16[16,64,4,64]{3,2,1,0:T(4,128)(2,1)S(1)} %copy-done.5, f32[64,4,16,16]{2,3,1,0:T(8,128)} %get-tuple-element.183, f32[64,4,16]{2,1,0:T(4,128)S(1)} %get-tuple-element.182), kind=kOutput, calls=%fused_computation.78 | convolution fusion | flops 9113615 | bytes 1589248 | tf_op jit(solution)/shard_map/nhts,tnhd->snhd/dot_general | solution.py:96
  73.0 6.1 %fusion.48 = bf16[16,64,4,64]{3,0,2,1:T(8,128)(2,1)} fusion(f32[64,4,16,16]{3,2,1,0:T(8,128)} %fusion.52, bf16[16,64,4,64]{3,2,1,0:T(4,128)(2,1)} %reshape.99, f32[64,4,16,16]{2,3,1,0:T(8,128)} %get-tuple-element.183, f32[64,4,16]{2,1,0:T(4,128)S(1)} %get-tuple-element.182), kind=kOutput, calls=%fused_computation.76 | convolution fusion | flops 9113615 | bytes 1589248 | tf_op jit(solution)/shard_map/nhts,snhd->tnhd/dot_general | solution.py:95
  79.2 3.5 %fusion.49 = bf16[16,64,4,64]{3,0,2,1:T(8,128)(2,1)} fusion(bf16[16,64,4,64]{3,2,1,0:T(4,128)(2,1)S(1)} %reshape_reshape.4, f32[64,4,16,16]{2,3,1,0:T(8,128)} %get-tuple-element.183, f32[64,4,16]{2,1,0:T(4,128)} %copy-done.13), kind=kOutput, calls=%fused_computation.77 | convolution fusion | flops 8781824 | bytes 1327104 | tf_op jit(solution)/shard_map/nhts,tnhd->snhd/dot_general | solution.py:89
  82.7 1.7 copy.63
  85.2 3.1 %copy.61 = bf16[16,64,4,64]{1,0,3,2:T(8,128)(2,1)S(1)} copy(bf16[16,64,4,64]{3,0,2,1:T(8,128)(2,1)} %fusion.48) | data formatting | bytes 1048576 | tf_op jit(solution)/shard_map/convert_element_type | solution.py:95
  89.0 2.9 %copy.65 = bf16[16,64,4,64]{1,0,3,2:T(8,128)(2,1)S(1)} copy(bf16[16,64,4,64]{3,0,2,1:T(8,128)(2,1)} %fusion.49) | data formatting | bytes 1048576 | tf_op jit(solution)/shard_map/convert_element_type | solution.py:89
  92.7 1.4 convolution_add_fusion.3
  95.6 3.5 %all-to-all-start.1 = ((bf16[16,64,256]{2,1,0:T(8,128)(2,1)}), bf16[16,64,256]{2,1,0:T(8,128)(2,1)S(1)}, u32[]{:S(2)}, u32[]{:S(2)}) async-start(bf16[16,64,256]{2,1,0:T(8,128)(2,1)} %bitcast.30), calls=%async_computation.1 | async-start | bytes 1048576 | tf_op jit(solution)/shard_map/all_to_all | solution.py:152
  101.3 10.9 %all-to-all-done.1 = bf16[16,64,256]{2,1,0:T(8,128)(2,1)S(1)} async-done(((bf16[16,64,256]{2,1,0:T(8,128)(2,1)}), bf16[16,64,256]{2,1,0:T(8,128)(2,1)S(1)}, u32[]{:S(2)}, u32[]{:S(2)}) %all-to-all-start.1) | async-done | bytes 524320 | tf_op jit(solution)/shard_map/all_to_all | solution.py:152
  113.1 18.6 %while.35 = (s32[]{:T(128)}, f32[4,256,256]{2,1,0:T(8,128)S(1)}, f32[4,256,256]{2,1,0:T(8,128)S(1)}, bf16[4,128,256]{2,1,0:T(8,128)(2,1)}, bf16[4,256,256]{2,1,0...) while((s32[]{:T(128)}, f32[4,256,256]{2,1,0:T(8,128)S(1)}, ...), condition=%wide.region_7.8_spmd.clone, body=%wide.region_6.7_spmd.sunk.clone | while | flops 370671616 | bytes 5576841 | solution.py:157
  133.7 2.3 collective-permute-done.1
  136.0 2.4 convolution_add_fusion.4
  138.5 125.3 %all-reduce.3.cloned.1.call-done = (f32[256,256]{1,0:T(8,128)}, f32[256,256]{1,0:T(8,128)}, f32[256,256]{1,0:T(8,128)}, f32[256,256]{1,0:T(8,128)}) async-done(((f32[256,256]{1,0:T(8,128)}, f32[256,256]{1,0:T(8,128)}, f32[256,256]{1,0:T(8,128)}, f32[256,256]{1,0:T(8,128)}), (f32[256,256]{1,0:T(8,128)}, f32[256,256]{1,0:T(8,128)}, f32[256,256]{1,0:T(8,128)}, ...) | async-done | bytes 1048592 | tf_op jit(solution)/shard_map/psum | solution.py:168
  263.8 1.7 copy.137
  265.5 1.7 copy.138
  267.1 1.7 copy.139
  268.8 1.7 copy.140
  (134 shorter events, 47.2 us)
Async XLA Ops:
  7.2 48.3 %copy-start = (bf16[256,256]{1,0:T(8,128)(2,1)S(1)}, bf16[256,256]{1,0:T(8,128)(2,1)}, u32[]{:S(2)}) copy-start(bf16[256,256]{1,0:T(8,128)(2,1)} %param.20) | copy-start | bytes 393220
  8.7 14.8 %copy-start.1 = (bf16[4,256,256]{2,1,0:T(8,128)(2,1)S(1)}, bf16[4,256,256]{2,1,0:T(8,128)(2,1)}, u32[]{:S(2)}) copy-start(bf16[4,256,256]{2,1,0:T(8,128)(2,1)} %param.14) | copy-start | bytes 1572868
  8.7 14.8 %copy-start.2 = (bf16[256,256]{1,0:T(8,128)(2,1)S(1)}, bf16[256,256]{1,0:T(8,128)(2,1)}, u32[]{:S(2)}) copy-start(bf16[256,256]{1,0:T(8,128)(2,1)} %param.19) | copy-start | bytes 393220
  15.9 7.4 %collective-permute-start = (bf16[4,128,256]{2,1,0:T(8,128)(2,1)S(1)}, bf16[4,128,256]{2,1,0:T(8,128)(2,1)S(1)}, u32[]{:S(2)}, u32[]{:S(2)}) collective-permute-start(bf16[4,128,256]{2,1,0:T(8,128)(2,1)S(1)} %select_select_fusion), channel_id=1, source_target_pairs={{0,1},{1,2},{2,3},{3,4},{4,5},{5,6},{6,7},{7,0},{8,9},{9,10},{10,1... | collective-permute-start | bytes 786440 | tf_op jit(solution)/shard_map/ppermute | solution.py:12
  35.6 1.2 copy-start.6
  35.6 19.8 %copy-start.12 = (bf16[4,256,256]{2,1,0:T(8,128)(2,1)}, bf16[4,256,256]{2,1,0:T(8,128)(2,1)S(1)}, u32[]{:S(2)}) copy-start(bf16[4,256,256]{2,1,0:T(8,128)(2,1)S(1)} %get-tuple-element.422) | copy-start | bytes 1572868
  35.6 6.8 %copy-start.4 = (bf16[16,1,1,64,256]{4,3,2,1,0:T(8,128)(2,1)S(1)}, bf16[16,1,1,64,256]{4,3,2,1,0:T(8,128)(2,1)}, u32[]{:S(2)}) copy-start(bf16[16,1,1,64,256]{4,3,2,1,0:T(8,128)(2,1)} %param.23) | copy-start | bytes 1572868
  36.9 18.5 %all-to-all-start = ((bf16[4,256,256]{2,0,1:T(4,128)(2,1)}), bf16[4,256,256]{2,0,1:T(4,128)(2,1)S(1)}, u32[]{:S(2)}, u32[]{:S(2)}) async-start(bf16[4,256,256]{2,0,1:T(4,128)(2,1)} %copy.52), calls=%async_computation | async-start | bytes 1048576 | tf_op jit(solution)/shard_map/all_to_all | solution.py:149
  55.4 1.8 copy-start.9
  55.8 3.1 %copy-start.8 = (bf16[256,256]{1,0:T(8,128)(2,1)S(1)}, bf16[256,256]{1,0:T(8,128)(2,1)}, u32[]{:S(2)}) copy-start(bf16[256,256]{1,0:T(8,128)(2,1)} %param.22) | copy-start | bytes 393220
  62.3 5.0 %copy-start.5 = (bf16[16,64,4,64]{3,2,1,0:T(4,128)(2,1)S(1)}, bf16[16,64,4,64]{3,2,1,0:T(4,128)(2,1)}, u32[]{:S(2)}) copy-start(bf16[16,64,4,64]{3,2,1,0:T(4,128)(2,1)} %reshape.100) | copy-start | bytes 1572868
  67.2 5.8 %copy-start.13 = (f32[64,4,16]{2,1,0:T(4,128)}, f32[64,4,16]{2,1,0:T(4,128)S(1)}, u32[]{:S(2)}) copy-start(f32[64,4,16]{2,1,0:T(4,128)S(1)} %get-tuple-element.182) | copy-start | bytes 49156
  79.2 3.5 %copy-start.7 = (bf16[16,64,4,64]{3,0,2,1:T(8,128)(2,1)S(1)}, bf16[16,64,4,64]{3,0,2,1:T(8,128)(2,1)}, u32[]{:S(2)}) copy-start(bf16[16,64,4,64]{3,0,2,1:T(8,128)(2,1)} %fusion.50) | copy-start | bytes 1572868
  92.7 1.5 copy-start.10
  95.6 16.5 %all-to-all-start.1 = ((bf16[16,64,256]{2,1,0:T(8,128)(2,1)}), bf16[16,64,256]{2,1,0:T(8,128)(2,1)S(1)}, u32[]{:S(2)}, u32[]{:S(2)}) async-start(bf16[16,64,256]{2,1,0:T(8,128)(2,1)} %bitcast.30), calls=%async_computation.1 | async-start | bytes 1048576 | tf_op jit(solution)/shard_map/all_to_all | solution.py:152
  99.1 164.7 %all-reduce.3.cloned.1.call-start = ((), (), s32[]{:S(2)}) async-start(), calls=%async_computation.2 | async-start | bytes 2097152 | tf_op jit(solution)/shard_map/psum | solution.py:168
  113.2 2.6 copy-start.3
  117.8 2.6 copy-start.3
  122.5 2.6 copy-start.3
  127.1 2.6 copy-start.3
  131.8 4.3 %copy-start.11 = (s32[4,128]{1,0:T(4,128)S(1)}, s32[4,128]{1,0:T(4,128)}, u32[]{:S(2)}) copy-start(s32[4,128]{1,0:T(4,128)} %param.17) | copy-start | bytes 6148
  131.8 4.3 %collective-permute-start.1 = (bf16[4,128,256]{2,1,0:T(8,128)(2,1)}, bf16[4,128,256]{2,1,0:T(8,128)(2,1)}, u32[]{:S(2)}, u32[]{:S(2)}) collective-permute-start(bf16[4,128,256]{2,1,0:T(8,128)(2,1)} %get-tuple-element.126), channel_id=1, source_target_pairs={{0,7},{1,0},{2,1},{3,2},{4,3},{5,4},{6,5},{7,6},{8,15},{9,8},{10,9... | collective-permute-start | bytes 786440 | tf_op jit(solution)/shard_map/ppermute | solution.py:12
Sparse Core Ops, SparseCore 0:
  133.8 129.9 all-reduce.2
where the time goes:
time: 278 us; the launch traced here: 277 us
  waiting for transfers between devices  158 us (57%)
  matrix products  53.5 us (19%)
  local copies, waits for them, and re-layouts  38.3 us (14%)
  between operations  14.4 us (5%)
  starting transfers between devices  9.7 us (3%)
  other arithmetic  3.06 us (1%)
    psum x1, waiting for transfers between devices, local(): lax.psum((grad_message, attn_grads[0], attn_grads[1], attn_grads[2]), ('d...  125 us
    all_to_all x1, waiting for transfers between devices, local(): lax.all_to_all(hidden, 'day', split_axis=1, concat_axis=0, tiled=True)  12.5 us
    all_to_all x1, waiting for transfers between devices, local(): lax.all_to_all(back, 'day', split_axis=0, concat_axis=1, tiled=True)  10.9 us
    ppermute x2, waiting for transfers between devices, from_behind(): return lax.ppermute(value, axis, pairs)  9.28 us
    gather x1, local copies, waits for them, and re-layouts, local(): picked = jnp.take_along_axis(node_states, halo_rows[:, :, None], axis=1)  7 us
    unnamed x30, local copies, waits for them, and re-layouts  6.74 us
    dot_general x1, matrix products, attend(): jnp.einsum('nhts,snhd->tnhd', score_f, key_f).astype(jnp.bfloat16)  6.14 us
    dot_general x1, matrix products, attend(): jnp.einsum('nhts,tnhd->snhd', score_f, query_f).astype(jnp.bfloat16)  5.79 us
  transfers between devices with their start and end apart: 5, of which 5 were waited for; matrix products, arithmetic and copies ran while one was open for 2% of the time, Pallas kernels for 0%

commit v1 on v0

--- a/solution.py
+++ b/solution.py
@@ -1,9 +1,19 @@
+import functools
 import jax
 import jax.numpy as jnp
 from jax import lax
 from jax.sharding import PartitionSpec as P
 
 HEADS = 4
+
+
+def plan_routes_all(raw, bus_axis, mesh_dim):
+    for d in (bus_axis, mesh_dim):
+        raw = jax.lax.psum(raw, d)
+    return raw
+
+
+assign_the_shapes = functools.partial(plan_routes_all, bus_axis="dom", mesh_dim="day")
 
 
 def from_behind(value, axis, steps):
@@ -165,8 +175,8 @@
     ).astype(jnp.bfloat16)
     scattered = jnp.einsum("dsn,dsh->dnh", slot_hot, returned, preferred_element_type=jnp.float32)
     state_grad = local_grad + scattered
-    grad_message, grad_query, grad_key, grad_value = lax.psum(
-        (grad_message, attn_grads[0], attn_grads[1], attn_grads[2]), ("day", "dom")
+    grad_message, grad_query, grad_key, grad_value = assign_the_shapes(
+        (grad_message, attn_grads[0], attn_grads[1], attn_grads[2])
     )
     return (state_grad, grad_message, grad_query, grad_key, grad_value)
 

time: 278 us -> 254 us (0.914)
  waiting for transfers between devices: 158 us -> 138 us
  local copies, waits for them, and re-layouts: 38.3 us -> 35 us
    psum x1 -> x2, waiting for transfers between devices: 125 us -> 105 us  [plan_routes_all(): raw = jax.lax.psum(raw, d)]
  transfers between devices with their start and end apart: 5 -> 6, of which waited for: 5 -> 6; matrix products, arithmetic and copies ran while one was open for 2% -> 2% of each run, Pallas kernels for 0% -> 0%
where the time goes in v1:
time: 254 us; the launch traced here: 253 us
  waiting for transfers between devices  138 us (54%)
  matrix products  52.2 us (21%)
  local copies, waits for them, and re-layouts  35 us (14%)
  between operations  14.4 us (6%)
  starting transfers between devices  9.74 us (4%)
  other arithmetic  3.08 us (1%)
    psum x2, waiting for transfers between devices, plan_routes_all(): raw = jax.lax.psum(raw, d)  105 us
    all_to_all x1, waiting for transfers between devices, local(): lax.all_to_all(hidden, 'day', split_axis=1, concat_axis=0, tiled=True)  12.5 us
    ppermute x2, waiting for transfers between devices, from_behind(): return lax.ppermute(value, axis, pairs)  10.8 us
    all_to_all x1, waiting for transfers between devices, local(): lax.all_to_all(back, 'day', split_axis=0, concat_axis=1, tiled=True)  9.83 us
    gather x1, local copies, waits for them, and re-layouts, local(): picked = jnp.take_along_axis(node_states, halo_rows[:, :, None], axis=1)  7 us
    unnamed x30, local copies, waits for them, and re-layouts  6.74 us
    dot_general x1, matrix products, attend(): jnp.einsum('nhts,snhd->tnhd', score_f, key_f).astype(jnp.bfloat16)  6.16 us
    dot_general x1, matrix products, attend(): jnp.einsum('nhts,tnhd->snhd', score_f, query_f).astype(jnp.bfloat16)  5.81 us
  transfers between devices with their start and end apart: 6, of which 6 were waited for; matrix products, arithmetic and copies ran while one was open for 2% of the time, Pallas kernels for 0%

profile of v1, /device:TPU:0, one launch (start us, length us, event | category | flops | bytes accessed | tf_op | source)
XLA Modules:
  0.0 253.2 jit_solution(2209630299610362486)
XLA Ops:
  8.7 7.0 %gather_fusion = bf16[512,256]{1,0:T(8,128)(2,1)S(1)} fusion(bf16[4,256,256]{2,1,0:T(8,128)(2,1)} %param.14, s32[512]{0:T(512)S(1)} %fusion.70), kind=kCustom, calls=%fused_computation | custom fusion | bytes 528384 | tf_op jit(solution)/shard_map/jit(take_along_axis)/gather | solution.py:147
  16.4 6.9 %collective-permute-done = bf16[4,128,256]{2,1,0:T(8,128)(2,1)S(1)} collective-permute-done((bf16[4,128,256]{2,1,0:T(8,128)(2,1)S(1)}, bf16[4,128,256]{2,1,0:T(8,128)(2,1)S(1)}, u32[]{:S(2)}, u32[]{:S(2)}) %collective-permute-start) | collective-permute-done | bytes 262176 | tf_op jit(solution)/shard_map/ppermute | solution.py:22
  23.4 12.2 %while.34 = (s32[]{:T(128)}, bf16[4,256,256]{2,1,0:T(8,128)(2,1)S(1)}, f32[4,256,256]{2,1,0:T(8,128)S(1)}, f32[4,256]{1,0:T(4,128)S(1)}, bf16[4,256,256]{2,1,0:T...) while((s32[]{:T(128)}, ...), condition=%wide.region_2.3_spmd.clone, body=%wide.region_0.2_spmd.sunk.clone | while | flops 287277312 | bytes 3111561 | solution.py:156
  36.8 5.6 %all-to-all-start = ((bf16[4,256,256]{2,0,1:T(4,128)(2,1)}), bf16[4,256,256]{2,0,1:T(4,128)(2,1)S(1)}, u32[]{:S(2)}, u32[]{:S(2)}) async-start(bf16[4,256,256]{2,0,1:T(4,128)(2,1)} %copy.52), calls=%async_computation | async-start | bytes 1048576 | tf_op jit(solution)/shard_map/all_to_all | solution.py:159
  42.9 12.5 %all-to-all-done = bf16[4,256,256]{2,0,1:T(4,128)(2,1)S(1)} async-done(((bf16[4,256,256]{2,0,1:T(4,128)(2,1)}), bf16[4,256,256]{2,0,1:T(4,128)(2,1)S(1)}, u32[]{:S(2)}, u32[]{:S(2)}) %all-to-all-start) | async-done | bytes 524320 | tf_op jit(solution)/shard_map/all_to_all | solution.py:159
  59.6 2.6 %fusion.52 = f32[64,4,16,16]{3,2,1,0:T(8,128)} fusion(bf16[16,64,4,64]{3,2,1,0:T(4,128)(2,1)S(1)} %reshape.101, bf16[16,64,4,64]{3,2,1,0:T(4,128)(2,1)S(1)} %reshape_reshape.4), kind=kOutput, calls=%fused_computation.87 | convolution fusion | flops 8388608 | bytes 1310720 | tf_op jit(solution)/shard_map/tnhd,snhd->nhts/dot_general | solution.py:100
  62.3 4.9 %fusion.77 = (f32[64,4,16]{2,1,0:T(4,128)S(1)}, f32[64,4,16,16]{2,3,1,0:T(8,128)}) fusion(pred[16,16]{0,1:T(8,128)(4,1)S(1)} %iota_compare_fusion.7, bf16[16,64,4,64]{3,2,1,0:T(4,128)(2,1)} %reshape.99, bf16[16,64,4,64]{3,2,1,0:T(4,128)(2,1)} %reshape.100), kind=kOutput, calls=%fused_computation.119 | convolution fusion | flops 8650767 | bytes 1327360 | tf_op jit(solution)/shard_map/sub | solution.py:95
  67.2 5.8 %fusion.50 = bf16[16,64,4,64]{3,0,2,1:T(8,128)(2,1)} fusion(f32[64,4,16,16]{3,2,1,0:T(8,128)} %fusion.52, bf16[16,64,4,64]{3,2,1,0:T(4,128)(2,1)S(1)} %copy-done.4, f32[64,4,16,16]{2,3,1,0:T(8,128)} %get-tuple-element.187, f32[64,4,16]{2,1,0:T(4,128)S(1)} %get-tuple-element.186), kind=kOutput, calls=%fused_computation.78 | convolution fusion | flops 9113615 | bytes 1589248 | tf_op jit(solution)/shard_map/nhts,tnhd->snhd/dot_general | solution.py:106
  73.0 6.2 %fusion.48 = bf16[16,64,4,64]{3,0,2,1:T(8,128)(2,1)} fusion(f32[64,4,16,16]{3,2,1,0:T(8,128)} %fusion.52, bf16[16,64,4,64]{3,2,1,0:T(4,128)(2,1)} %reshape.99, f32[64,4,16,16]{2,3,1,0:T(8,128)} %get-tuple-element.187, f32[64,4,16]{2,1,0:T(4,128)S(1)} %get-tuple-element.186), kind=kOutput, calls=%fused_computation.76 | convolution fusion | flops 9113615 | bytes 1589248 | tf_op jit(solution)/shard_map/nhts,snhd->tnhd/dot_general | solution.py:105
  79.2 3.5 %fusion.49 = bf16[16,64,4,64]{3,0,2,1:T(8,128)(2,1)} fusion(bf16[16,64,4,64]{3,2,1,0:T(4,128)(2,1)S(1)} %reshape_reshape.4, f32[64,4,16,16]{2,3,1,0:T(8,128)} %get-tuple-element.187, f32[64,4,16]{2,1,0:T(4,128)} %copy-done.12), kind=kOutput, calls=%fused_computation.77 | convolution fusion | flops 8781824 | bytes 1327104 | tf_op jit(solution)/shard_map/nhts,tnhd->snhd/dot_general | solution.py:99
  82.7 1.7 copy.63
  85.2 3.1 %copy.61 = bf16[16,64,4,64]{1,0,3,2:T(8,128)(2,1)S(1)} copy(bf16[16,64,4,64]{3,0,2,1:T(8,128)(2,1)} %fusion.48) | data formatting | bytes 1048576 | tf_op jit(solution)/shard_map/convert_element_type | solution.py:105
  89.1 2.9 %copy.65 = bf16[16,64,4,64]{1,0,3,2:T(8,128)(2,1)S(1)} copy(bf16[16,64,4,64]{3,0,2,1:T(8,128)(2,1)} %fusion.49) | data formatting | bytes 1048576 | tf_op jit(solution)/shard_map/convert_element_type | solution.py:99
  95.7 3.5 %all-to-all-start.1 = ((bf16[16,64,256]{2,1,0:T(8,128)(2,1)}), bf16[16,64,256]{2,1,0:T(8,128)(2,1)S(1)}, u32[]{:S(2)}, u32[]{:S(2)}) async-start(bf16[16,64,256]{2,1,0:T(8,128)(2,1)} %bitcast.30), calls=%async_computation.1 | async-start | bytes 1048576 | tf_op jit(solution)/shard_map/all_to_all | solution.py:162
  102.3 9.8 %all-to-all-done.1 = bf16[16,64,256]{2,1,0:T(8,128)(2,1)S(1)} async-done(((bf16[16,64,256]{2,1,0:T(8,128)(2,1)}), bf16[16,64,256]{2,1,0:T(8,128)(2,1)S(1)}, u32[]{:S(2)}, u32[]{:S(2)}) %all-to-all-start.1) | async-done | bytes 524320 | tf_op jit(solution)/shard_map/all_to_all | solution.py:162
  112.4 15.7 %while.35 = (s32[]{:T(128)}, f32[4,256,256]{2,1,0:T(8,128)S(1)}, f32[4,256,256]{2,1,0:T(8,128)S(1)}, bf16[4,128,256]{2,1,0:T(8,128)(2,1)S(1)}, bf16[4,256,256]{2...) while((s32[]{:T(128)}, f32[4,256,256]{2,1,0:T(8,128)S(1)}, ...), condition=%wide.region_7.8_spmd.clone, body=%wide.region_6.7_spmd.sunk.clone | while | flops 370671616 | bytes 3479153 | solution.py:167
  129.0 56.0 %all-reduce.5.cloned.1.call-done = (f32[256,256]{1,0:T(8,128)}, f32[256,256]{1,0:T(8,128)}, f32[256,256]{1,0:T(8,128)}, f32[256,256]{1,0:T(8,128)}) async-done(((f32[256,256]{1,0:T(8,128)}, f32[256,256]{1,0:T(8,128)}, f32[256,256]{1,0:T(8,128)}, f32[256,256]{1,0:T(8,128)}), (f32[256,256]{1,0:T(8,128)}, f32[256,256]{1,0:T(8,128)}, f32[256,256]{1,0:T(8,128)}, ...) | async-done | bytes 1048592 | tf_op jit(solution)/shard_map/psum | solution.py:12
  185.1 3.9 %collective-permute-done.1 = bf16[4,128,256]{2,1,0:T(8,128)(2,1)S(1)} collective-permute-done((bf16[4,128,256]{2,1,0:T(8,128)(2,1)S(1)}, bf16[4,128,256]{2,1,0:T(8,128)(2,1)S(1)}, u32[]{:S(2)}, u32[]{:S(2)}) %collective-permute-start.1) | collective-permute-done | bytes 262176 | tf_op jit(solution)/shard_map/ppermute | solution.py:22
  189.0 1.5 convolution_add_fusion.4
  190.5 49.2 %all-reduce.7.cloned.1.call-done = (f32[256,256]{1,0:T(8,128)}, f32[256,256]{1,0:T(8,128)}, f32[256,256]{1,0:T(8,128)}, f32[256,256]{1,0:T(8,128)}) async-done(((f32[256,256]{1,0:T(8,128)}, f32[256,256]{1,0:T(8,128)}, f32[256,256]{1,0:T(8,128)}, f32[256,256]{1,0:T(8,128)}), (f32[256,256]{1,0:T(8,128)}, f32[256,256]{1,0:T(8,128)}, f32[256,256]{1,0:T(8,128)}, ...) | async-done | bytes 1048592 | tf_op jit(solution)/shard_map/psum | solution.py:12
  239.7 1.7 copy.141
  241.3 1.7 copy.142
  243.0 1.7 copy.143
  244.7 1.7 copy.144
  (129 shorter events, 45.0 us)
Async XLA Ops:
  7.2 48.3 %copy-start = (bf16[256,256]{1,0:T(8,128)(2,1)S(1)}, bf16[256,256]{1,0:T(8,128)(2,1)}, u32[]{:S(2)}) copy-start(bf16[256,256]{1,0:T(8,128)(2,1)} %param.20) | copy-start | bytes 393220
  8.7 14.8 %copy-start.1 = (bf16[4,256,256]{2,1,0:T(8,128)(2,1)S(1)}, bf16[4,256,256]{2,1,0:T(8,128)(2,1)}, u32[]{:S(2)}) copy-start(bf16[4,256,256]{2,1,0:T(8,128)(2,1)} %param.14) | copy-start | bytes 1572868
  8.7 14.8 %copy-start.2 = (bf16[256,256]{1,0:T(8,128)(2,1)S(1)}, bf16[256,256]{1,0:T(8,128)(2,1)}, u32[]{:S(2)}) copy-start(bf16[256,256]{1,0:T(8,128)(2,1)} %param.19) | copy-start | bytes 393220
  15.9 7.4 %collective-permute-start = (bf16[4,128,256]{2,1,0:T(8,128)(2,1)S(1)}, bf16[4,128,256]{2,1,0:T(8,128)(2,1)S(1)}, u32[]{:S(2)}, u32[]{:S(2)}) collective-permute-start(bf16[4,128,256]{2,1,0:T(8,128)(2,1)S(1)} %select_select_fusion), channel_id=1, source_target_pairs={{0,1},{1,2},{2,3},{3,4},{4,5},{5,6},{6,7},{7,0},{8,9},{9,10},{10,1... | collective-permute-start | bytes 786440 | tf_op jit(solution)/shard_map/ppermute | solution.py:22
  35.6 1.2 copy-start.5
  35.6 19.8 %copy-start.11 = (bf16[4,256,256]{2,1,0:T(8,128)(2,1)}, bf16[4,256,256]{2,1,0:T(8,128)(2,1)S(1)}, u32[]{:S(2)}) copy-start(bf16[4,256,256]{2,1,0:T(8,128)(2,1)S(1)} %get-tuple-element.426) | copy-start | bytes 1572868
  35.6 6.8 %copy-start.3 = (bf16[16,1,1,64,256]{4,3,2,1,0:T(8,128)(2,1)S(1)}, bf16[16,1,1,64,256]{4,3,2,1,0:T(8,128)(2,1)}, u32[]{:S(2)}) copy-start(bf16[16,1,1,64,256]{4,3,2,1,0:T(8,128)(2,1)} %param.23) | copy-start | bytes 1572868
  36.8 18.5 %all-to-all-start = ((bf16[4,256,256]{2,0,1:T(4,128)(2,1)}), bf16[4,256,256]{2,0,1:T(4,128)(2,1)S(1)}, u32[]{:S(2)}, u32[]{:S(2)}) async-start(bf16[4,256,256]{2,0,1:T(4,128)(2,1)} %copy.52), calls=%async_computation | async-start | bytes 1048576 | tf_op jit(solution)/shard_map/all_to_all | solution.py:159
  55.4 1.8 copy-start.8
  55.8 3.1 %copy-start.7 = (bf16[256,256]{1,0:T(8,128)(2,1)S(1)}, bf16[256,256]{1,0:T(8,128)(2,1)}, u32[]{:S(2)}) copy-start(bf16[256,256]{1,0:T(8,128)(2,1)} %param.22) | copy-start | bytes 393220
  62.2 4.9 %copy-start.4 = (bf16[16,64,4,64]{3,2,1,0:T(4,128)(2,1)S(1)}, bf16[16,64,4,64]{3,2,1,0:T(4,128)(2,1)}, u32[]{:S(2)}) copy-start(bf16[16,64,4,64]{3,2,1,0:T(4,128)(2,1)} %reshape.100) | copy-start | bytes 1572868
  67.2 5.8 %copy-start.12 = (f32[64,4,16]{2,1,0:T(4,128)}, f32[64,4,16]{2,1,0:T(4,128)S(1)}, u32[]{:S(2)}) copy-start(f32[64,4,16]{2,1,0:T(4,128)S(1)} %get-tuple-element.186) | copy-start | bytes 49156
  79.2 3.5 %copy-start.6 = (bf16[16,64,4,64]{3,0,2,1:T(8,128)(2,1)S(1)}, bf16[16,64,4,64]{3,0,2,1:T(8,128)(2,1)}, u32[]{:S(2)}) copy-start(bf16[16,64,4,64]{3,0,2,1:T(8,128)(2,1)} %fusion.50) | copy-start | bytes 1572868
  92.7 1.5 copy-start.9
  95.7 16.5 %all-to-all-start.1 = ((bf16[16,64,256]{2,1,0:T(8,128)(2,1)}), bf16[16,64,256]{2,1,0:T(8,128)(2,1)S(1)}, u32[]{:S(2)}, u32[]{:S(2)}) async-start(bf16[16,64,256]{2,1,0:T(8,128)(2,1)} %bitcast.30), calls=%async_computation.1 | async-start | bytes 1048576 | tf_op jit(solution)/shard_map/all_to_all | solution.py:162
  99.1 85.9 %all-reduce.5.cloned.1.call-start = ((), (), s32[]{:S(2)}) async-start(), calls=%async_computation.2 | async-start | bytes 2097152 | tf_op jit(solution)/shard_map/psum | solution.py:12
  128.1 60.9 %copy-start.10 = (s32[4,128]{1,0:T(4,128)S(1)}, s32[4,128]{1,0:T(4,128)}, u32[]{:S(2)}) copy-start(s32[4,128]{1,0:T(4,128)} %param.17) | copy-start | bytes 6148
  128.9 110.7 %all-reduce.7.cloned.1.call-start = ((), (), s32[]{:S(2)}) async-start(), calls=%async_computation.3 | async-start | bytes 2097152 | tf_op jit(solution)/shard_map/psum | solution.py:12
  185.0 3.9 %collective-permute-start.1 = (bf16[4,128,256]{2,1,0:T(8,128)(2,1)S(1)}, bf16[4,128,256]{2,1,0:T(8,128)(2,1)S(1)}, u32[]{:S(2)}, u32[]{:S(2)}) collective-permute-start(bf16[4,128,256]{2,1,0:T(8,128)(2,1)S(1)} %get-tuple-element.126), channel_id=1, source_target_pairs={{0,7},{1,0},{2,1},{3,2},{4,3},{5,4},{6,5},{7,6},{8,15},{9,8},{10,9... | collective-permute-start | bytes 786440 | tf_op jit(solution)/shard_map/ppermute | solution.py:22
Sparse Core Ops, SparseCore 0:
  129.0 55.9 all-reduce.4
  187.6 52.0 all-reduce.6
